TPU v7x, 32 devices: a whole 2x2x4 slice. The times are simulated.
32 devices in a mesh: dp: 16 (over z, y, core), ctx: 2 (over x).
Axes of the slice: x: 2, y: 2, z: 4, core: 2. Of those that a mesh axis runs over, the one named last changes fastest.
Arguments:
- tokens: bfloat16 [16, 2, 384, 8192], P('dp', 'ctx'), may hold values from -6 to 6
- lengths: int32 [16, 2], P('dp'), may hold values from 96 to 384, as said below
- norm_gain: float32 [8192], replicated, may hold values from 0.5 to 1.5
- w_in: bfloat16 [8192, 1536], P('dp'), may hold values from -0.0625 to 0.0625
- short_filter: float32 [3, 1536], replicated, may hold values from -3.5 to 3.5
- decay_rate: float32 [16, 512], replicated, may hold values from 5e-05 to 0.03
- residue: float32 [16, 512], replicated, may hold values from -0.12 to 0.12
- skip_gain: float32 [512], replicated, may hold values from -6 to 6
- w_out: bfloat16 [512, 8192], P(None, 'dp'), may hold values from -0.25 to 0.25
- steer_table: float32 [50, 2, 8192], replicated, may hold values from -3 to 3
- steer_layer: int32 [16], P('dp'), may hold values from 0 to 49
- steer_slab: int32 [16], P('dp'), may hold values from 0 to 7
Outputs:
- result: bfloat16 [16, 2, 384, 8192], P('dp', 'ctx')
Inputs may be any that keep to these rules, and one draw needn't show every extreme that they name: `lengths`: each group holds 96 to 384 live tokens; in every sequence one group holds exactly 384.
All inputs are finite; a program needn't handle non-finite values.
Results may differ from a plain program's by a relative error of at most 0.004.
The roundings to bfloat16 on the way count: a program that leaves them out, or rounds other values in their place, can miss the bound.
Values may be sent and summed in bfloat16 or wider, within the bound.
No kernel may reach another device: no remote copies, remote signals or barrier semaphores. Data moves between devices by JAX's collectives and lax.ppermute only.
A program may use at most 192 MiB of HBM per device.

v0:
```python
import jax
import jax.numpy as jnp
from jax import lax
from jax.sharding import PartitionSpec as P

STEER_W = 1024
BLOCK = 32


def from_behind(value, axis, steps):
    count = lax.axis_size(axis)
    first, last = (max(0, -steps), min(count, count - steps))
    return lax.ppermute(value, axis, [(source, source + steps) for source in range(first, last)])


def normalize(rows_in, gain):
    values = rows_in.astype(jnp.float32)
    scale = lax.rsqrt(jnp.mean(values * values, axis=1, keepdims=True) + 1e-06)
    return (values * scale * gain[None, :]).astype(jnp.bfloat16)


def filter_tables(decay_rate, residue, block):
    lags = jnp.arange(block)
    lags_float = lags.astype(jnp.float32)
    taps = jnp.sum(residue[None] * jnp.exp(-decay_rate[None] * lags_float[:, None, None]), axis=1)
    diff = lags[:, None] - lags[None, :]
    toeplitz = jnp.where((diff >= 0)[:, :, None], taps[jnp.clip(diff, 0, block - 1)], 0.0)
    toeplitz = jnp.transpose(toeplitz, (1, 0, 2))
    lead = residue[:, None] * jnp.exp(-decay_rate[:, None] * (lags_float + 1.0)[None, :, None])
    close = jnp.exp(-decay_rate[None] * (block - 1 - lags_float)[:, None, None])
    return (toeplitz, lead, close)


def block_states(drive, decay_rate, close, block):
    cap, width = drive.shape
    count = cap // block
    pieces = drive.reshape(count, block, width)
    ends = jnp.sum(close[None] * pieces[:, :, None, :], axis=1)
    steps = jnp.arange(count)
    gap = (steps[:, None] - steps[None, :]).astype(jnp.float32)
    powers = jnp.where(
        (gap >= 0)[:, :, None, None],
        jnp.exp(-decay_rate[None, None] * (block * jnp.maximum(gap, 0.0))[:, :, None, None]),
        0.0,
    )
    return jnp.sum(powers * ends[None], axis=1)


def block_outputs(drive, states, incoming, decay_rate, toeplitz, lead, block):
    cap, width = drive.shape
    count = cap // block
    pieces = drive.reshape(count, block, width)
    inside = jnp.sum(toeplitz[None] * pieces[:, :, None, :], axis=1)
    starts = (jnp.arange(count) * block).astype(jnp.float32)
    carried = incoming[None] * jnp.exp(-decay_rate[None] * starts[:, None, None])
    before = jnp.concatenate([jnp.zeros_like(states[:1]), states[:-1]], axis=0) + carried
    earlier = jnp.sum(lead[None] * before[:, :, None, :], axis=1)
    return (inside + earlier).reshape(cap, width)


def per_device(
    tokens,
    lengths,
    norm_gain,
    w_in,
    short_filter,
    decay_rate,
    residue,
    skip_gain,
    w_out,
    steer_table,
    steer_layer,
    steer_slab,
):
    cap = tokens.shape[2]
    width = tokens.shape[3]
    slab = residue.shape[1]
    groups = lax.axis_size("ctx")
    rows_in = tokens.reshape(cap, width)
    normed = normalize(rows_in, norm_gain)
    position = lax.axis_index("ctx")
    group_lens = lengths.reshape(-1)
    own_len = lax.dynamic_index_in_dim(group_lens, position, 0, keepdims=False)
    live = jnp.arange(cap) < own_len
    own_tail = lax.dynamic_slice_in_dim(normed, own_len - 2, 2, 0)
    tail_normed = from_behind(own_tail, "ctx", 1)
    block = BLOCK if cap % BLOCK == 0 else cap
    toeplitz, lead, close = filter_tables(decay_rate, residue, block)
    lens_f = group_lens.astype(jnp.float32)
    cumlen = jnp.cumsum(lens_f)
    rescale = jnp.exp(decay_rate * (cap - own_len).astype(jnp.float32))
    piece = jnp.concatenate([w_in, w_out.T], axis=1)
    gathered = lax.all_gather(piece, "dp", axis=0, tiled=True)
    w_in_all = gathered[:, : 3 * slab]
    w_out_t = gathered[:, 3 * slab :]
    rows_ext = jnp.concatenate([tail_normed, normed], axis=0)
    extended = jnp.dot(rows_ext, w_in_all, preferred_element_type=jnp.float32)
    extended = lax.reduce_precision(extended, exponent_bits=8, mantissa_bits=7)
    feat = (
        short_filter[0] * extended[2:]
        + short_filter[1] * extended[1:-1]
        + short_filter[2] * extended[:-2]
    )
    gate = feat[:, :slab]
    drive = jnp.where(live[:, None], feat[:, slab : 2 * slab] * feat[:, 2 * slab :], 0.0)
    states = block_states(drive, decay_rate, close, block)
    ending = states[-1] * rescale
    incoming = jnp.zeros_like(ending)
    for k in range(1, groups):
        got = from_behind(ending, "ctx", k)
        source = position - k
        between = lax.dynamic_index_in_dim(
            cumlen, jnp.maximum(position - 1, 0), 0, keepdims=False
        ) - lax.dynamic_index_in_dim(cumlen, jnp.maximum(source, 0), 0, keepdims=False)
        weight = jnp.where(source >= 0, jnp.exp(-decay_rate * between), 0.0)
        incoming = incoming + weight * got
    local = block_outputs(drive, states, incoming, decay_rate, toeplitz, lead, block)
    filtered = local + skip_gain[None, :] * drive
    gated = jnp.where(live[:, None], gate * filtered, 0.0).astype(jnp.bfloat16)
    mixed = lax.dot_general(
        gated, w_out_t, (((1,), (1,)), ((), ())), preferred_element_type=jnp.float32
    )
    rows2 = lax.dynamic_index_in_dim(steer_table, steer_layer[0], 0, keepdims=False)
    shift_vec = rows2[0] - rows2[1]
    columns = jnp.arange(width) // STEER_W
    steer = jnp.where(columns == steer_slab[0], 2.0 * shift_vec, 0.0)
    summed = rows_in.astype(jnp.float32) + mixed + steer[None, :]
    summed = jnp.where(live[:, None], summed, 0.0)
    return summed.astype(jnp.bfloat16).reshape(tokens.shape)


def solution(mesh):
    placed = (
        P("dp", "ctx", None, None),
        P("dp", None),
        P(),
        P("dp", None),
        P(),
        P(),
        P(),
        P(),
        P(None, "dp"),
        P(),
        P("dp"),
        P("dp"),
    )
    return jax.shard_map(
        per_device,
        mesh=mesh,
        in_specs=placed,
        out_specs=P("dp", "ctx", None, None),
        check_vma=False,
    )
```

profile of v0, /device:TPU:0, one launch (start us, length us, event | category | flops | bytes accessed | tf_op | source)
XLA Modules:
  0.0 229.9 jit_solution(1049465095491891067)
XLA Ops:
  6.5 0.0 all-gather.2.cloned.1.call-start
  6.5 1.3 copy.17
  7.8 0.0 copy-start.5
  7.8 3.0 %pad_maximum_fusion = bf16[512,2048]{1,0:T(8,128)(2,1)} fusion(bf16[512,512]{1,0:T(8,128)(2,1)S(1)} %copy.17, bf16[512,1536]{1,0:T(8,128)(2,1)} %param.15), kind=kLoop, calls=%fused_computation.27 | loop fusion | flops 4194304 | bytes 4194304 | tf_op jit(solution)/shard_map/concatenate | solution.py:92
  10.9 0.0 all-gather.2.cloned.1.call-update
  10.9 0.0 copy-done.13
  10.9 0.7 constant_dynamic-slice_fusion.2
  12.9 4.1 %fusion.2 = f32[384]{0:T(512)S(1)} fusion(bf16[1,1,384,8192]{3,2,1,0:T(8,128)(2,1)} %param.12), kind=kLoop, calls=%fused_computation.7 | loop fusion | flops 9436800 | bytes 6292992 | tf_op jit(solution)/shard_map/reduce_sum | solution.py:18
  17.1 0.0 copy-done.5
  17.1 0.0 copy-start.3
  17.1 0.0 copy-start.4
  17.1 4.7 %fusion.4 = bf16[384,8192]{1,0:T(8,128)(2,1)S(1)} fusion(bf16[1,1,384,8192]{3,2,1,0:T(8,128)(2,1)} %param.12, f32[8192]{0:T(1024)S(1)} %copy-done.5, f32[384]{0:T(512)S(1)} %add_rsqrt_fusion), kind=kLoop, calls=%fused_computation.9 | loop fusion | flops 12582912 | bytes 12617216 | tf_op jit(solution)/shard_map/convert_element_type | solution.py:19
  21.8 0.0 copy-start.1
  21.8 2.7 %copy-done.1 = bf16[384,8192]{1,0:T(8,128)(2,1)} copy-done((bf16[384,8192]{1,0:T(8,128)(2,1)}, bf16[384,8192]{1,0:T(8,128)(2,1)S(1)}, u32[]{:S(2)}) %copy-start.1) | copy-done | bytes 6291480
  24.5 0.1 constant_dynamic-slice_fusion.1
  24.6 5.7 %collective-permute-start = (bf16[2,8192]{1,0:T(2,128)(2,1)S(1)}, bf16[2,8192]{1,0:T(2,128)(2,1)S(1)}, u32[]{:S(2)}, u32[]{:S(2)}) collective-permute-start(bf16[2,8192]{1,0:T(2,128)(2,1)S(1)} %constant_dynamic-slice_fusion.1), channel_id=1, source_target_pairs={{0,1},{2,3},{4,5},{6,7},{8,9},{10,11},{12,13},{14,15},{16,17},{18,... | collective-permute-start | bytes 98312 | tf_op jit(solution)/shard_map/ppermute | solution.py:13
  30.3 0.0 copy-done.3
  30.3 0.1 reshape.177
  31.7 0.0 copy-done.4
  31.7 1.4 multiply_exponential_fusion
  33.2 4.8 %gather_fusion = f32[1024,512]{1,0:T(8,128)} fusion(f32[32,512]{1,0:T(8,128)S(1)} %get-tuple-element.9, s32[1024]{0:T(1024)S(1)} %broadcast_clamp_fusion), kind=kCustom, calls=%fused_computation | custom fusion | bytes 4198400 | tf_op jit(solution)/shard_map/gather | solution.py:27
  38.0 1.3 iota_compare_fusion
  39.3 0.6 convert_compare_fusion
  39.9 0.6 maximum_multiply_fusion
  40.5 0.0 copy-done.6
  40.5 0.6 slice_reduce_fusion.2
  41.2 1.0 fusion.26
  42.1 0.2 exponential_multiply_fusion
  42.4 1.8 broadcast_select_fusion
  44.2 0.6 multiply_convert_fusion
  45.5 2.6 %copy.18 = f32[32,32,512]{2,1,0:T(8,128)} copy(f32[32,32,512]{2,0,1:T(8,128)S(1)} %broadcast_select_fusion) | data formatting | bytes 4194304 | tf_op jit(solution)/shard_map/jit(_where)/select_n | solution.py:27
  48.1 0.2 reduce-window.4
  48.2 0.7 fusion.31
  48.9 0.0 collective-permute-done
  48.9 0.6 copy-done.12
  49.5 132.3 %all-gather.2.cloned.1.call-done = bf16[8192,2048]{1,0:T(8,128)(2,1)} async-done(((bf16[512,2048]{1,0:T(8,128)(2,1)}), bf16[8192,2048]{1,0:T(8,128)(2,1)}) %all-gather.2.cloned.1.call-update) | async-done | bytes 33554448 | tf_op jit(solution)/shard_map/all_gather | solution.py:93
  181.8 16.7 %fusion.13 = f32[386,1536]{1,0:T(8,128)S(1)} fusion(bf16[8192,2048]{1,0:T(8,128)(2,1)} %all-gather.2.cloned.1.call-done, bf16[384,8192]{1,0:T(8,128)(2,1)} %copy-done.1, bf16[2,8192]{1,0:T(2,128)(2,1)} %copy-done.12), kind=kOutput, calls=%fused_computation.21 | convolution fusion | flops 9727249408 | bytes 33861632 | tf_op jit(solution)/shard_map/dot_general | solution.py:97
  198.5 0.0 copy-start.9
  198.6 0.0 copy-start.2
  198.6 0.0 copy-start.7
  198.6 0.0 copy-start.10
  198.6 0.0 copy-start
  198.6 1.6 fusion.18
  200.2 0.0 copy-done.9
  200.2 0.0 copy-start.11
  200.2 0.1 fusion.20
  200.3 0.0 copy-done.2
  200.3 1.1 multiply_reduce_fusion.2
  201.4 0.0 copy-done.7
  201.4 0.0 copy-done.10
  201.4 0.0 copy-start.8
  201.4 1.3 multiply_reduce_fusion.3
  202.8 3.6 %collective-permute-start.1 = (f32[16,512]{1,0:T(8,128)S(1)}, f32[16,512]{1,0:T(8,128)S(1)}, u32[]{:S(2)}, u32[]{:S(2)}) collective-permute-start(f32[16,512]{1,0:T(8,128)S(1)} %fusion.27), channel_id=1, source_target_pairs={{0,1},{2,3},{4,5},{6,7},{8,9},{10,11},{12,13},{14,15},{16,17},{18,... | collective-permute-start | bytes 98312 | tf_op jit(solution)/shard_map/ppermute | solution.py:13
  206.4 0.0 copy-done
  206.4 2.4 %multiply_reduce_fusion = f32[12,32,512]{2,1,0:T(8,128)S(1)} fusion(f32[12,32,512]{2,1,0:T(8,128)S(1)} %bitcast.36, f32[32,32,512]{2,1,0:T(8,128)S(1)} %copy-done), kind=kLoop, calls=%fused_computation.3 | loop fusion | flops 12386304 | bytes 3670016 | tf_op jit(solution)/shard_map/reduce_sum | solution.py:53
  208.9 0.0 collective-permute-done.1
  208.9 0.7 select_multiply_fusion
  209.6 0.0 copy-done.11
  209.6 0.1 multiply_add_fusion
  209.8 1.0 multiply_reduce_fusion.1
  210.8 0.1 add.100
  210.9 0.0 copy-done.8
  210.9 0.2 fusion.22
  211.2 11.9 %fusion.8 = bf16[1,1,384,8192]{3,2,1,0:T(8,128)(2,1)} fusion(bf16[384,512]{1,0:T(8,128)(2,1)S(1)} %fusion.22, bf16[8192,2048]{1,0:T(8,128)(2,1)} %all-gather.2.cloned.1.call-done, bf16[1,1,384,8192]{3,2,1,0:T(8,128)(2,1)} %param.12, f32[8192]{0:T(1024)S(1)} %fusion.29, pred[384]{0:T(512)(128)(4,1)S(1)} %copy-done.9), kind=kOutput, calls=%fused_computation.15 | convolution fusion | flops 3236954112 | bytes 21397888 | tf_op jit(solution)/shard_map/dot_general | solution.py:120
  (15 shorter events, 0.1 us)
Async XLA Ops:
  6.5 4.4 %copy-start.13 = (s32[1,2]{1,0:T(1,128)S(1)}, s32[1,2]{1,0:T(1,128)}, u32[]{:S(2)}) copy-start(s32[1,2]{1,0:T(1,128)} %param.13) | copy-start | bytes 28
  6.5 175.3 %all-gather.2.cloned.1.call-start = ((), (), s32[]{:S(2)}) async-start(), calls=%async_computation | async-start | bytes 35651584 | tf_op jit(solution)/shard_map/all_gather | solution.py:93
  7.8 9.3 %copy-start.5 = (f32[8192]{0:T(1024)S(1)}, f32[8192]{0:T(1024)}, u32[]{:S(2)}) copy-start(f32[8192]{0:T(1024)} %param.14) | copy-start | bytes 98308
  17.1 13.2 %copy-start.3 = (f32[16,512]{1,0:T(8,128)S(1)}, f32[16,512]{1,0:T(8,128)}, u32[]{:S(2)}) copy-start(f32[16,512]{1,0:T(8,128)} %param.17) | copy-start | bytes 98308
  17.1 14.6 %copy-start.4 = (f32[16,512]{1,0:T(8,128)S(1)}, f32[16,512]{1,0:T(8,128)}, u32[]{:S(2)}) copy-start(f32[16,512]{1,0:T(8,128)} %param.18) | copy-start | bytes 98308
  21.8 2.7 %copy-start.1 = (bf16[384,8192]{1,0:T(8,128)(2,1)}, bf16[384,8192]{1,0:T(8,128)(2,1)S(1)}, u32[]{:S(2)}) copy-start(bf16[384,8192]{1,0:T(8,128)(2,1)S(1)} %fusion.4) | copy-start | bytes 18874372
  24.6 24.3 %collective-permute-start = (bf16[2,8192]{1,0:T(2,128)(2,1)S(1)}, bf16[2,8192]{1,0:T(2,128)(2,1)S(1)}, u32[]{:S(2)}, u32[]{:S(2)}) collective-permute-start(bf16[2,8192]{1,0:T(2,128)(2,1)S(1)} %constant_dynamic-slice_fusion.1), channel_id=1, source_target_pairs={{0,1},{2,3},{4,5},{6,7},{8,9},{10,11},{12,13},{14,15},{16,17},{18,... | collective-permute-start | bytes 98312 | tf_op jit(solution)/shard_map/ppermute | solution.py:13
  33.2 7.3 %copy-start.6 = (f32[3,1536]{1,0:T(4,128)S(1)}, f32[3,1536]{1,0:T(4,128)}, u32[]{:S(2)}) copy-start(f32[3,1536]{1,0:T(4,128)} %param.16) | copy-start | bytes 55300
  48.9 0.6 copy-start.12
  198.5 1.6 copy-start.9
  198.6 1.8 copy-start.2
  198.6 2.9 %copy-start.7 = (f32[12,12]{1,0:T(8,128)S(1)}, f32[12,12]{1,0:T(8,128)}, u32[]{:S(2)}) copy-start(f32[12,12]{1,0:T(8,128)} %maximum_multiply_fusion) | copy-start | bytes 1732
  198.6 2.9 %copy-start.10 = (pred[12,12]{1,0:T(8,128)(4,1)S(1)}, pred[12,12]{1,0:T(8,128)(4,1)}, u32[]{:S(2)}) copy-start(pred[12,12]{1,0:T(8,128)(4,1)} %convert_compare_fusion) | copy-start | bytes 436
  198.6 7.8 %copy-start = (f32[32,32,512]{2,1,0:T(8,128)S(1)}, f32[32,32,512]{2,1,0:T(8,128)}, u32[]{:S(2)}) copy-start(f32[32,32,512]{2,1,0:T(8,128)} %copy.18) | copy-start | bytes 6291460
  200.2 9.4 %copy-start.11 = (f32[12]{0:T(128)S(1)}, f32[12]{0:T(128)}, u32[]{:S(2)}) copy-start(f32[12]{0:T(128)} %multiply_convert_fusion) | copy-start | bytes 148
  201.4 9.5 %copy-start.8 = (f32[512]{0:T(512)S(1)}, f32[512]{0:T(512)}, u32[]{:S(2)}) copy-start(f32[512]{0:T(512)} %param.19) | copy-start | bytes 6148
  202.8 6.1 %collective-permute-start.1 = (f32[16,512]{1,0:T(8,128)S(1)}, f32[16,512]{1,0:T(8,128)S(1)}, u32[]{:S(2)}, u32[]{:S(2)}) collective-permute-start(f32[16,512]{1,0:T(8,128)S(1)} %fusion.27), channel_id=1, source_target_pairs={{0,1},{2,3},{4,5},{6,7},{8,9},{10,11},{12,13},{14,15},{16,17},{18,... | collective-permute-start | bytes 98312 | tf_op jit(solution)/shard_map/ppermute | solution.py:13
Sparse Core Ops, SparseCore 0:
  11.0 170.7 all-gather.1
where the time goes:
time: 230 us
  waiting for transfers between devices  132 us (57%)
  other arithmetic  29.1 us (13%)
  matrix products  28.7 us (12%)
  between operations  17.2 us (7%)
  local copies, waits for them, and re-layouts  13.5 us (6%)
  starting transfers between devices  9.25 us (4%)
    all_gather x1, waiting for transfers between devices, per_device(): gathered = lax.all_gather(piece, 'dp', axis=0, tiled=True)  132 us
    dot_general x1, matrix products, per_device(): extended = jnp.dot(rows_ext, w_in_all, preferred_element_type=jnp.float32)  16.7 us
    dot_general x1, matrix products, per_device(): lax.dot_general(gated, w_out_t, (((1,), (1,)), ((), ())), preferred_eleme...  11.9 us
    ppermute x2, starting transfers between devices, from_behind(): lax.ppermute(value, axis, [(source, source + steps) for source in range(f...  9.25 us
    gather x1, local copies, waits for them, and re-layouts, filter_tables(): taps[jnp.clip(diff, 0, block - 1)]  4.84 us
    convert_element_type x1, other arithmetic, normalize(): return (values * scale * gain[None, :]).astype(jnp.bfloat16)  4.73 us
  transfers between devices with their start and end apart: 3, of which 1 were waited for; matrix products, arithmetic and copies ran while one was open for 12% of the time, Pallas kernels for 0%

commit v1 on v0

--- a/solution.py
+++ b/solution.py
@@ -5,6 +5,16 @@
 
 STEER_W = 1024
 BLOCK = 32
+
+
+def around_the_ring(x, mesh_axis, dim):
+    devices = lax.axis_size(mesh_axis)
+    held, parts = (x, [x])
+    for _ in range(devices - 1):
+        held = lax.ppermute(held, mesh_axis, [(i, (i + 1) % devices) for i in range(devices)])
+        parts.insert(0, held)
+    row_of_blocks = jnp.concatenate(parts, axis=dim)
+    return jnp.roll(row_of_blocks, (lax.axis_index(mesh_axis) + 1) * x.shape[dim], axis=dim)
 
 
 def from_behind(value, axis, steps):
@@ -90,7 +100,7 @@
     cumlen = jnp.cumsum(lens_f)
     rescale = jnp.exp(decay_rate * (cap - own_len).astype(jnp.float32))
     piece = jnp.concatenate([w_in, w_out.T], axis=1)
-    gathered = lax.all_gather(piece, "dp", axis=0, tiled=True)
+    gathered = around_the_ring(piece, "dp", 0)
     w_in_all = gathered[:, : 3 * slab]
     w_out_t = gathered[:, 3 * slab :]
     rows_ext = jnp.concatenate([tail_normed, normed], axis=0)

time: 230 us -> 546 us (2.37)
  waiting for transfers between devices: 132 us -> 392 us
  local copies, waits for them, and re-layouts: 13.5 us -> 84.4 us
  between operations: 17.2 us -> 3.76 us
    ppermute x0 -> x15, waiting for transfers between devices: none -> 392 us  [around_the_ring(): lax.ppermute(held, mesh_axis, [(i, (i + 1) % devices) for i in range(devi...]
    all_gather x1 -> x0, waiting for transfers between devices: 132 us -> none  [per_device(): gathered = lax.all_gather(piece, 'dp', axis=0, tiled=True)]
    unnamed x28 -> x92, local copies, waits for them, and re-layouts: 3.36 us -> 74.2 us
  transfers between devices with their start and end apart: 3 -> 17, of which waited for: 1 -> 15; matrix products, arithmetic and copies ran while one was open for 12% -> 17% of each run, Pallas kernels for 0% -> 0%
where the time goes in v1:
time: 546 us
  waiting for transfers between devices  392 us (72%)
  local copies, waits for them, and re-layouts  84.4 us (15%)
  other arithmetic  29.9 us (5%)
  matrix products  27.7 us (5%)
  starting transfers between devices  8.21 us (2%)
    ppermute x15, waiting for transfers between devices, around_the_ring(): lax.ppermute(held, mesh_axis, [(i, (i + 1) % devices) for i in range(devi...  392 us
    unnamed x92, local copies, waits for them, and re-layouts  74.2 us
    dot_general x1, matrix products, per_device(): extended = jnp.dot(rows_ext, w_in_all, preferred_element_type=jnp.float32)  15.7 us
    dot_general x1, matrix products, per_device(): lax.dot_general(gated, w_out_t, (((1,), (1,)), ((), ())), preferred_eleme...  12 us
  transfers between devices with their start and end apart: 17, of which 15 were waited for; matrix products, arithmetic and copies ran while one was open for 17% of the time, Pallas kernels for 0%

profile of v1, /device:TPU:0, one launch (start us, length us, event | category | flops | bytes accessed | tf_op | source)
XLA Modules:
  0.0 545.7 jit_solution(3431432635606216492)
XLA Ops:
  1.3 1.7 pad_maximum_fusion
  3.4 28.7 %collective-permute-done.1 = bf16[512,2048]{1,0:T(8,128)(2,1)S(1)} collective-permute-done((bf16[512,2048]{1,0:T(8,128)(2,1)S(1)}, bf16[512,2048]{1,0:T(8,128)(2,1)S(1)}, u32[]{:S(2)}, u32[]{:S(2)}) %collective-permute-start.1) | collective-permute-done | bytes 2097184 | tf_op jit(solution)/shard_map/ppermute | solution.py:14
  33.5 28.2 %collective-permute-done.2 = bf16[512,2048]{1,0:T(8,128)(2,1)S(1)} collective-permute-done((bf16[512,2048]{1,0:T(8,128)(2,1)S(1)}, bf16[512,2048]{1,0:T(8,128)(2,1)S(1)}, u32[]{:S(2)}, u32[]{:S(2)}) %collective-permute-start.2) | collective-permute-done | bytes 2097184 | tf_op jit(solution)/shard_map/ppermute | solution.py:14
  63.0 28.2 %collective-permute-done.3 = bf16[512,2048]{1,0:T(8,128)(2,1)S(1)} collective-permute-done((bf16[512,2048]{1,0:T(8,128)(2,1)S(1)}, bf16[512,2048]{1,0:T(8,128)(2,1)S(1)}, u32[]{:S(2)}, u32[]{:S(2)}) %collective-permute-start.3) | collective-permute-done | bytes 2097184 | tf_op jit(solution)/shard_map/ppermute | solution.py:14
  91.1 1.4 copy-done.6
  92.5 28.2 %collective-permute-done.4 = bf16[512,2048]{1,0:T(8,128)(2,1)S(1)} collective-permute-done((bf16[512,2048]{1,0:T(8,128)(2,1)S(1)}, bf16[512,2048]{1,0:T(8,128)(2,1)S(1)}, u32[]{:S(2)}, u32[]{:S(2)}) %collective-permute-start.4) | collective-permute-done | bytes 2097184 | tf_op jit(solution)/shard_map/ppermute | solution.py:14
  120.7 1.4 copy-done.8
  122.0 28.2 %collective-permute-done.5 = bf16[512,2048]{1,0:T(8,128)(2,1)S(1)} collective-permute-done((bf16[512,2048]{1,0:T(8,128)(2,1)S(1)}, bf16[512,2048]{1,0:T(8,128)(2,1)S(1)}, u32[]{:S(2)}, u32[]{:S(2)}) %collective-permute-start.5) | collective-permute-done | bytes 2097184 | tf_op jit(solution)/shard_map/ppermute | solution.py:14
  150.2 1.4 copy-done.10
  151.6 28.2 %collective-permute-done.6 = bf16[512,2048]{1,0:T(8,128)(2,1)S(1)} collective-permute-done((bf16[512,2048]{1,0:T(8,128)(2,1)S(1)}, bf16[512,2048]{1,0:T(8,128)(2,1)S(1)}, u32[]{:S(2)}, u32[]{:S(2)}) %collective-permute-start.6) | collective-permute-done | bytes 2097184 | tf_op jit(solution)/shard_map/ppermute | solution.py:14
  181.1 28.2 %collective-permute-done.7 = bf16[512,2048]{1,0:T(8,128)(2,1)S(1)} collective-permute-done((bf16[512,2048]{1,0:T(8,128)(2,1)S(1)}, bf16[512,2048]{1,0:T(8,128)(2,1)S(1)}, u32[]{:S(2)}, u32[]{:S(2)}) %collective-permute-start.7) | collective-permute-done | bytes 2097184 | tf_op jit(solution)/shard_map/ppermute | solution.py:14
  210.6 28.2 %collective-permute-done.8 = bf16[512,2048]{1,0:T(8,128)(2,1)S(1)} collective-permute-done((bf16[512,2048]{1,0:T(8,128)(2,1)S(1)}, bf16[512,2048]{1,0:T(8,128)(2,1)S(1)}, u32[]{:S(2)}, u32[]{:S(2)}) %collective-permute-start.8) | collective-permute-done | bytes 2097184 | tf_op jit(solution)/shard_map/ppermute | solution.py:14
  240.1 28.2 %collective-permute-done.9 = bf16[512,2048]{1,0:T(8,128)(2,1)S(1)} collective-permute-done((bf16[512,2048]{1,0:T(8,128)(2,1)S(1)}, bf16[512,2048]{1,0:T(8,128)(2,1)S(1)}, u32[]{:S(2)}, u32[]{:S(2)}) %collective-permute-start.9) | collective-permute-done | bytes 2097184 | tf_op jit(solution)/shard_map/ppermute | solution.py:14
  269.6 28.2 %collective-permute-done.10 = bf16[512,2048]{1,0:T(8,128)(2,1)S(1)} collective-permute-done((bf16[512,2048]{1,0:T(8,128)(2,1)S(1)}, bf16[512,2048]{1,0:T(8,128)(2,1)S(1)}, u32[]{:S(2)}, u32[]{:S(2)}) %collective-permute-start.10) | collective-permute-done | bytes 2097184 | tf_op jit(solution)/shard_map/ppermute | solution.py:14
  297.7 1.4 copy-done.20
  299.1 28.2 %collective-permute-done.11 = bf16[512,2048]{1,0:T(8,128)(2,1)S(1)} collective-permute-done((bf16[512,2048]{1,0:T(8,128)(2,1)S(1)}, bf16[512,2048]{1,0:T(8,128)(2,1)S(1)}, u32[]{:S(2)}, u32[]{:S(2)}) %collective-permute-start.11) | collective-permute-done | bytes 2097184 | tf_op jit(solution)/shard_map/ppermute | solution.py:14
  329.8 4.1 fusion.2
  333.9 21.6 %collective-permute-done.12 = bf16[512,2048]{1,0:T(8,128)(2,1)} collective-permute-done((bf16[512,2048]{1,0:T(8,128)(2,1)S(1)}, bf16[512,2048]{1,0:T(8,128)(2,1)}, u32[]{:S(2)}, u32[]{:S(2)}) %collective-permute-start.12) | collective-permute-done | bytes 2097184 | tf_op jit(solution)/shard_map/ppermute | solution.py:14
  355.5 4.7 fusion.4
  360.3 23.7 %collective-permute-done.13 = bf16[512,2048]{1,0:T(8,128)(2,1)} collective-permute-done((bf16[512,2048]{1,0:T(8,128)(2,1)}, bf16[512,2048]{1,0:T(8,128)(2,1)}, u32[]{:S(2)}, u32[]{:S(2)}) %collective-permute-start.13) | collective-permute-done | bytes 2097184 | tf_op jit(solution)/shard_map/ppermute | solution.py:14
  384.1 3.8 collective-permute-start
  388.0 1.5 multiply_exponential_fusion
  389.5 4.9 gather_fusion
  394.4 1.8 broadcast_select_fusion
  396.2 16.3 %collective-permute-done.14 = bf16[512,2048]{1,0:T(8,128)(2,1)} collective-permute-done((bf16[512,2048]{1,0:T(8,128)(2,1)}, bf16[512,2048]{1,0:T(8,128)(2,1)}, u32[]{:S(2)}, u32[]{:S(2)}) %collective-permute-start.14) | collective-permute-done | bytes 2097184 | tf_op jit(solution)/shard_map/ppermute | solution.py:14
  413.1 2.6 copy.18
  421.0 19.9 %collective-permute-done.15 = bf16[512,2048]{1,0:T(8,128)(2,1)} collective-permute-done((bf16[512,2048]{1,0:T(8,128)(2,1)}, bf16[512,2048]{1,0:T(8,128)(2,1)}, u32[]{:S(2)}, u32[]{:S(2)}) %collective-permute-start.15) | collective-permute-done | bytes 2097184 | tf_op jit(solution)/shard_map/ppermute | solution.py:14
  440.9 3.2 constant_dynamic-update-slice_fusion.31
  444.1 3.3 constant_dynamic-update-slice_fusion.30
  447.4 3.3 constant_dynamic-update-slice_fusion.29
  450.8 3.3 constant_dynamic-update-slice_fusion.28
  454.1 1.6 constant_dynamic-update-slice_fusion.27
  455.8 1.5 constant_dynamic-update-slice_fusion.26
  457.2 1.6 constant_dynamic-update-slice_fusion.25
  458.8 1.6 constant_dynamic-update-slice_fusion.24
  460.4 1.6 constant_dynamic-update-slice_fusion.23
  462.0 1.6 constant_dynamic-update-slice_fusion.22
  463.5 1.6 constant_dynamic-update-slice_fusion.21
  465.1 1.6 constant_dynamic-update-slice_fusion.20
  466.8 1.6 constant_dynamic-update-slice_fusion.19
  468.4 1.6 constant_dynamic-update-slice_fusion.18
  470.0 1.6 constant_dynamic-update-slice_fusion.17
  471.6 1.6 constant_dynamic-update-slice_fusion.16
  473.2 3.1 constant_dynamic-update-slice_fusion.15
  476.3 3.2 constant_dynamic-update-slice_fusion.14
  479.5 3.1 constant_dynamic-update-slice_fusion.13
  482.7 3.2 constant_dynamic-update-slice_fusion.12
  485.9 1.6 constant_dynamic-update-slice_fusion.11
  487.5 1.4 constant_dynamic-update-slice_fusion.10
  488.9 1.6 constant_dynamic-update-slice_fusion.9
  490.5 1.6 constant_dynamic-update-slice_fusion.8
  492.1 1.6 constant_dynamic-update-slice_fusion.7
  493.6 1.6 constant_dynamic-update-slice_fusion.6
  495.3 1.6 constant_dynamic-update-slice_fusion.5
  496.8 1.6 constant_dynamic-update-slice_fusion.4
  498.4 1.6 constant_dynamic-update-slice_fusion.3
  500.1 1.6 constant_dynamic-update-slice_fusion.2
  501.6 1.6 constant_dynamic-update-slice_fusion.1
  503.2 1.6 constant_dynamic-update-slice_fusion
  504.8 15.7 %fusion.13 = f32[386,1536]{1,0:T(8,128)S(1)} fusion(bf16[16384,2048]{1,0:T(8,128)(2,1)} %constant_dynamic-update-slice_fusion, s32[]{:T(128)S(6)} %select_n.85, bf16[384,8192]{1,0:T(8,128)(2,1)} %copy-done.24, bf16[2,8192]{1,0:T(2,128)(2,1)S(1)} %collective-permute-done), kind=kOutput, calls=%fused_computation.21 | convolution fusion | flops 9727249408 | bytes 33861636 | tf_op jit(solution)/shard_map/dot_general | solution.py:107
  521.4 2.4 multiply_reduce_fusion.2
  525.1 3.8 collective-permute-start.16
  529.0 2.4 multiply_reduce_fusion
  533.7 12.0 %fusion.8 = bf16[1,1,384,8192]{3,2,1,0:T(8,128)(2,1)} fusion(bf16[384,512]{1,0:T(8,128)(2,1)S(1)} %fusion.22, bf16[16384,2048]{1,0:T(8,128)(2,1)} %constant_dynamic-update-slice_fusion, s32[]{:T(128)S(6)} %select_n.85, s32[]{:T(128)S(6)} %add.126, bf16[1,1,384,8192]{3,2,1,0:T(8,128)(2,1)} %param.12, f32[8192]{0:T(1024)S(1)} %fusion.29, ...), kind=kOutput, calls=%fused_computation.15 | convolution fusion | flops 3236954112 | bytes 21397896 | tf_op jit(solution)/shard_map/dot_general | solution.py:130
  (108 shorter events, 19.6 us)
Async XLA Ops:
  0.0 387.9 %copy-start.26 = (f32[16,512]{1,0:T(8,128)S(1)}, f32[16,512]{1,0:T(8,128)}, u32[]{:S(2)}) copy-start(f32[16,512]{1,0:T(8,128)} %param.17) | copy-start | bytes 98308
  0.0 388.0 %copy-start.27 = (f32[16,512]{1,0:T(8,128)S(1)}, f32[16,512]{1,0:T(8,128)}, u32[]{:S(2)}) copy-start(f32[16,512]{1,0:T(8,128)} %param.18) | copy-start | bytes 98308
  2.9 29.2 %collective-permute-start.1 = (bf16[512,2048]{1,0:T(8,128)(2,1)S(1)}, bf16[512,2048]{1,0:T(8,128)(2,1)S(1)}, u32[]{:S(2)}, u32[]{:S(2)}) collective-permute-start(bf16[512,2048]{1,0:T(8,128)(2,1)S(1)} %pad_maximum_fusion), channel_id=1, source_target_pairs={{0,2},{2,4},{4,6},{6,8},{8,10},{10,12},{12,14},{14,16},{16,18},{18... | collective-permute-start | bytes 6291464 | tf_op jit(solution)/shard_map/ppermute | solution.py:14
  32.1 1.3 copy-start.2
  33.5 28.2 %collective-permute-start.2 = (bf16[512,2048]{1,0:T(8,128)(2,1)S(1)}, bf16[512,2048]{1,0:T(8,128)(2,1)S(1)}, u32[]{:S(2)}, u32[]{:S(2)}) collective-permute-start(bf16[512,2048]{1,0:T(8,128)(2,1)S(1)} %collective-permute-done.1), channel_id=1, source_target_pairs={{0,2},{2,4},{4,6},{6,8},{8,10},{10,12},{12,14},{14,16},{16,18},{18... | collective-permute-start | bytes 6291464 | tf_op jit(solution)/shard_map/ppermute | solution.py:14
  61.6 1.3 copy-start.4
  63.0 28.2 %collective-permute-start.3 = (bf16[512,2048]{1,0:T(8,128)(2,1)S(1)}, bf16[512,2048]{1,0:T(8,128)(2,1)S(1)}, u32[]{:S(2)}, u32[]{:S(2)}) collective-permute-start(bf16[512,2048]{1,0:T(8,128)(2,1)S(1)} %collective-permute-done.2), channel_id=1, source_target_pairs={{0,2},{2,4},{4,6},{6,8},{8,10},{10,12},{12,14},{14,16},{16,18},{18... | collective-permute-start | bytes 6291464 | tf_op jit(solution)/shard_map/ppermute | solution.py:14
  91.1 1.4 copy-start.6
  92.5 28.2 %collective-permute-start.4 = (bf16[512,2048]{1,0:T(8,128)(2,1)S(1)}, bf16[512,2048]{1,0:T(8,128)(2,1)S(1)}, u32[]{:S(2)}, u32[]{:S(2)}) collective-permute-start(bf16[512,2048]{1,0:T(8,128)(2,1)S(1)} %collective-permute-done.3), channel_id=1, source_target_pairs={{0,2},{2,4},{4,6},{6,8},{8,10},{10,12},{12,14},{14,16},{16,18},{18... | collective-permute-start | bytes 6291464 | tf_op jit(solution)/shard_map/ppermute | solution.py:14
  120.7 1.4 copy-start.8
  122.0 28.2 %collective-permute-start.5 = (bf16[512,2048]{1,0:T(8,128)(2,1)S(1)}, bf16[512,2048]{1,0:T(8,128)(2,1)S(1)}, u32[]{:S(2)}, u32[]{:S(2)}) collective-permute-start(bf16[512,2048]{1,0:T(8,128)(2,1)S(1)} %collective-permute-done.4), channel_id=1, source_target_pairs={{0,2},{2,4},{4,6},{6,8},{8,10},{10,12},{12,14},{14,16},{16,18},{18... | collective-permute-start | bytes 6291464 | tf_op jit(solution)/shard_map/ppermute | solution.py:14
  150.2 1.4 copy-start.10
  151.6 28.2 %collective-permute-start.6 = (bf16[512,2048]{1,0:T(8,128)(2,1)S(1)}, bf16[512,2048]{1,0:T(8,128)(2,1)S(1)}, u32[]{:S(2)}, u32[]{:S(2)}) collective-permute-start(bf16[512,2048]{1,0:T(8,128)(2,1)S(1)} %collective-permute-done.5), channel_id=1, source_target_pairs={{0,2},{2,4},{4,6},{6,8},{8,10},{10,12},{12,14},{14,16},{16,18},{18... | collective-permute-start | bytes 6291464 | tf_op jit(solution)/shard_map/ppermute | solution.py:14
  179.7 1.3 copy-start.12
  181.1 28.2 %collective-permute-start.7 = (bf16[512,2048]{1,0:T(8,128)(2,1)S(1)}, bf16[512,2048]{1,0:T(8,128)(2,1)S(1)}, u32[]{:S(2)}, u32[]{:S(2)}) collective-permute-start(bf16[512,2048]{1,0:T(8,128)(2,1)S(1)} %collective-permute-done.6), channel_id=1, source_target_pairs={{0,2},{2,4},{4,6},{6,8},{8,10},{10,12},{12,14},{14,16},{16,18},{18... | collective-permute-start | bytes 6291464 | tf_op jit(solution)/shard_map/ppermute | solution.py:14
  209.2 1.3 copy-start.14
  210.6 28.2 %collective-permute-start.8 = (bf16[512,2048]{1,0:T(8,128)(2,1)S(1)}, bf16[512,2048]{1,0:T(8,128)(2,1)S(1)}, u32[]{:S(2)}, u32[]{:S(2)}) collective-permute-start(bf16[512,2048]{1,0:T(8,128)(2,1)S(1)} %collective-permute-done.7), channel_id=1, source_target_pairs={{0,2},{2,4},{4,6},{6,8},{8,10},{10,12},{12,14},{14,16},{16,18},{18... | collective-permute-start | bytes 6291464 | tf_op jit(solution)/shard_map/ppermute | solution.py:14
  238.7 1.3 copy-start.16
  240.1 28.2 %collective-permute-start.9 = (bf16[512,2048]{1,0:T(8,128)(2,1)S(1)}, bf16[512,2048]{1,0:T(8,128)(2,1)S(1)}, u32[]{:S(2)}, u32[]{:S(2)}) collective-permute-start(bf16[512,2048]{1,0:T(8,128)(2,1)S(1)} %collective-permute-done.8), channel_id=1, source_target_pairs={{0,2},{2,4},{4,6},{6,8},{8,10},{10,12},{12,14},{14,16},{16,18},{18... | collective-permute-start | bytes 6291464 | tf_op jit(solution)/shard_map/ppermute | solution.py:14
  268.2 1.3 copy-start.18
  269.6 28.2 %collective-permute-start.10 = (bf16[512,2048]{1,0:T(8,128)(2,1)S(1)}, bf16[512,2048]{1,0:T(8,128)(2,1)S(1)}, u32[]{:S(2)}, u32[]{:S(2)}) collective-permute-start(bf16[512,2048]{1,0:T(8,128)(2,1)S(1)} %collective-permute-done.9), channel_id=1, source_target_pairs={{0,2},{2,4},{4,6},{6,8},{8,10},{10,12},{12,14},{14,16},{16,18},{18... | collective-permute-start | bytes 6291464 | tf_op jit(solution)/shard_map/ppermute | solution.py:14
  297.7 1.4 copy-start.20
  299.1 28.2 %collective-permute-start.11 = (bf16[512,2048]{1,0:T(8,128)(2,1)S(1)}, bf16[512,2048]{1,0:T(8,128)(2,1)S(1)}, u32[]{:S(2)}, u32[]{:S(2)}) collective-permute-start(bf16[512,2048]{1,0:T(8,128)(2,1)S(1)} %collective-permute-done.10), channel_id=1, source_target_pairs={{0,2},{2,4},{4,6},{6,8},{8,10},{10,12},{12,14},{14,16},{16,18},{18... | collective-permute-start | bytes 6291464 | tf_op jit(solution)/shard_map/ppermute | solution.py:14
  327.3 60.8 %copy-start.22 = (bf16[512,2048]{1,0:T(8,128)(2,1)}, bf16[512,2048]{1,0:T(8,128)(2,1)S(1)}, u32[]{:S(2)}) copy-start(bf16[512,2048]{1,0:T(8,128)(2,1)S(1)} %collective-permute-done.11) | copy-start | bytes 6291460
  327.3 28.3 %collective-permute-start.12 = (bf16[512,2048]{1,0:T(8,128)(2,1)S(1)}, bf16[512,2048]{1,0:T(8,128)(2,1)}, u32[]{:S(2)}, u32[]{:S(2)}) collective-permute-start(bf16[512,2048]{1,0:T(8,128)(2,1)S(1)} %collective-permute-done.11), channel_id=1, source_target_pairs={{0,2},{2,4},{4,6},{6,8},{8,10},{10,12},{12,14},{14,16},{16,18},{18... | collective-permute-start | bytes 6291464 | tf_op jit(solution)/shard_map/ppermute | solution.py:14
  355.5 28.5 %collective-permute-start.13 = (bf16[512,2048]{1,0:T(8,128)(2,1)}, bf16[512,2048]{1,0:T(8,128)(2,1)}, u32[]{:S(2)}, u32[]{:S(2)}) collective-permute-start(bf16[512,2048]{1,0:T(8,128)(2,1)} %collective-permute-done.12), channel_id=1, source_target_pairs={{0,2},{2,4},{4,6},{6,8},{8,10},{10,12},{12,14},{14,16},{16,18},{18... | collective-permute-start | bytes 6291464 | tf_op jit(solution)/shard_map/ppermute | solution.py:14
  360.3 23.7 %copy-start.24 = (bf16[384,8192]{1,0:T(8,128)(2,1)}, bf16[384,8192]{1,0:T(8,128)(2,1)S(1)}, u32[]{:S(2)}) copy-start(bf16[384,8192]{1,0:T(8,128)(2,1)S(1)} %fusion.4) | copy-start | bytes 18874372
  360.3 52.2 %copy-start.30 = (s32[1,2]{1,0:T(1,128)S(1)}, s32[1,2]{1,0:T(1,128)}, u32[]{:S(2)}) copy-start(s32[1,2]{1,0:T(1,128)} %param.13) | copy-start | bytes 28
  384.0 28.5 %collective-permute-start.14 = (bf16[512,2048]{1,0:T(8,128)(2,1)}, bf16[512,2048]{1,0:T(8,128)(2,1)}, u32[]{:S(2)}, u32[]{:S(2)}) collective-permute-start(bf16[512,2048]{1,0:T(8,128)(2,1)} %collective-permute-done.13), channel_id=1, source_target_pairs={{0,2},{2,4},{4,6},{6,8},{8,10},{10,12},{12,14},{14,16},{16,18},{18... | collective-permute-start | bytes 6291464 | tf_op jit(solution)/shard_map/ppermute | solution.py:14
  384.1 120.7 %collective-permute-start = (bf16[2,8192]{1,0:T(2,128)(2,1)S(1)}, bf16[2,8192]{1,0:T(2,128)(2,1)S(1)}, u32[]{:S(2)}, u32[]{:S(2)}) collective-permute-start(bf16[2,8192]{1,0:T(2,128)(2,1)S(1)} %constant_dynamic-slice_fusion.1), channel_id=1, source_target_pairs={{0,1},{2,3},{4,5},{6,7},{8,9},{10,11},{12,13},{14,15},{16,17},{18,... | collective-permute-start | bytes 98312 | tf_op jit(solution)/shard_map/ppermute | solution.py:23
  389.5 29.3 %copy-start.28 = (f32[3,1536]{1,0:T(4,128)S(1)}, f32[3,1536]{1,0:T(4,128)}, u32[]{:S(2)}) copy-start(f32[3,1536]{1,0:T(4,128)} %param.16) | copy-start | bytes 55300
  412.5 28.5 %collective-permute-start.15 = (bf16[512,2048]{1,0:T(8,128)(2,1)}, bf16[512,2048]{1,0:T(8,128)(2,1)}, u32[]{:S(2)}, u32[]{:S(2)}) collective-permute-start(bf16[512,2048]{1,0:T(8,128)(2,1)} %collective-permute-done.14), channel_id=1, source_target_pairs={{0,2},{2,4},{4,6},{6,8},{8,10},{10,12},{12,14},{14,16},{16,18},{18... | collective-permute-start | bytes 6291464 | tf_op jit(solution)/shard_map/ppermute | solution.py:14
  415.7 40.0 %copy-start.21 = (bf16[512,2048]{1,0:T(8,128)(2,1)S(1)}, bf16[512,2048]{1,0:T(8,128)(2,1)}, u32[]{:S(2)}) copy-start(bf16[512,2048]{1,0:T(8,128)(2,1)} %copy-done.20) | copy-start | bytes 6291460
  418.0 36.2 %copy-start.23 = (bf16[512,2048]{1,0:T(8,128)(2,1)S(1)}, bf16[512,2048]{1,0:T(8,128)(2,1)}, u32[]{:S(2)}) copy-start(bf16[512,2048]{1,0:T(8,128)(2,1)} %copy-done.22) | copy-start | bytes 6291460
  421.0 36.2 %copy-start.19 = (bf16[512,2048]{1,0:T(8,128)(2,1)S(1)}, bf16[512,2048]{1,0:T(8,128)(2,1)}, u32[]{:S(2)}) copy-start(bf16[512,2048]{1,0:T(8,128)(2,1)} %copy-done.18) | copy-start | bytes 6291460
  444.1 14.7 %copy-start.17 = (bf16[512,2048]{1,0:T(8,128)(2,1)S(1)}, bf16[512,2048]{1,0:T(8,128)(2,1)}, u32[]{:S(2)}) copy-start(bf16[512,2048]{1,0:T(8,128)(2,1)} %copy-done.16) | copy-start | bytes 6291460
  447.4 13.0 %copy-start.15 = (bf16[512,2048]{1,0:T(8,128)(2,1)S(1)}, bf16[512,2048]{1,0:T(8,128)(2,1)}, u32[]{:S(2)}) copy-start(bf16[512,2048]{1,0:T(8,128)(2,1)} %copy-done.14) | copy-start | bytes 6291460
  450.8 11.2 %copy-start.13 = (bf16[512,2048]{1,0:T(8,128)(2,1)S(1)}, bf16[512,2048]{1,0:T(8,128)(2,1)}, u32[]{:S(2)}) copy-start(bf16[512,2048]{1,0:T(8,128)(2,1)} %copy-done.12) | copy-start | bytes 6291460
  454.1 9.4 %copy-start.11 = (bf16[512,2048]{1,0:T(8,128)(2,1)S(1)}, bf16[512,2048]{1,0:T(8,128)(2,1)}, u32[]{:S(2)}) copy-start(bf16[512,2048]{1,0:T(8,128)(2,1)} %copy-done.10) | copy-start | bytes 6291460
  455.7 9.4 %copy-start.9 = (bf16[512,2048]{1,0:T(8,128)(2,1)S(1)}, bf16[512,2048]{1,0:T(8,128)(2,1)}, u32[]{:S(2)}) copy-start(bf16[512,2048]{1,0:T(8,128)(2,1)} %copy-done.8) | copy-start | bytes 6291460
  457.2 9.5 %copy-start.7 = (bf16[512,2048]{1,0:T(8,128)(2,1)S(1)}, bf16[512,2048]{1,0:T(8,128)(2,1)}, u32[]{:S(2)}) copy-start(bf16[512,2048]{1,0:T(8,128)(2,1)} %copy-done.6) | copy-start | bytes 6291460
  458.8 9.6 %copy-start.5 = (bf16[512,2048]{1,0:T(8,128)(2,1)S(1)}, bf16[512,2048]{1,0:T(8,128)(2,1)}, u32[]{:S(2)}) copy-start(bf16[512,2048]{1,0:T(8,128)(2,1)} %copy-done.4) | copy-start | bytes 6291460
  460.4 9.6 %copy-start.3 = (bf16[512,2048]{1,0:T(8,128)(2,1)S(1)}, bf16[512,2048]{1,0:T(8,128)(2,1)}, u32[]{:S(2)}) copy-start(bf16[512,2048]{1,0:T(8,128)(2,1)} %copy-done.2) | copy-start | bytes 6291460
  462.0 9.6 %copy-start = (bf16[512,1536]{1,0:T(8,128)(2,1)S(1)}, bf16[512,1536]{1,0:T(8,128)(2,1)}, u32[]{:S(2)}) copy-start(bf16[512,1536]{1,0:T(8,128)(2,1)} %param.15) | copy-start | bytes 4718596
  520.5 8.5 %copy-start.1 = (f32[32,32,512]{2,1,0:T(8,128)S(1)}, f32[32,32,512]{2,1,0:T(8,128)}, u32[]{:S(2)}) copy-start(f32[32,32,512]{2,1,0:T(8,128)} %copy.18) | copy-start | bytes 6291460
  520.5 11.7 %copy-start.25 = (f32[16,32,512]{2,1,0:T(8,128)S(1)}, f32[16,32,512]{2,1,0:T(8,128)}, u32[]{:S(2)}) copy-start(f32[16,32,512]{2,1,0:T(8,128)} %exponential_multiply_fusion) | copy-start | bytes 3145732
  520.5 12.9 %copy-start.29 = (f32[512]{0:T(512)S(1)}, f32[512]{0:T(512)}, u32[]{:S(2)}) copy-start(f32[512]{0:T(512)} %param.19) | copy-start | bytes 6148
  525.1 6.3 %collective-permute-start.16 = (f32[16,512]{1,0:T(8,128)S(1)}, f32[16,512]{1,0:T(8,128)S(1)}, u32[]{:S(2)}, u32[]{:S(2)}) collective-permute-start(f32[16,512]{1,0:T(8,128)S(1)} %fusion.27), channel_id=1, source_target_pairs={{0,1},{2,3},{4,5},{6,7},{8,9},{10,11},{12,13},{14,15},{16,17},{18,... | collective-permute-start | bytes 98312 | tf_op jit(solution)/shard_map/ppermute | solution.py:23
